TPU v7x, 256 devices: a whole 4x4x8 slice. The times are simulated.
256 devices in a mesh: expert: 128 (over x, z, y), hid: 2 (over core).
Axes of the slice: x: 4, y: 4, z: 8, core: 2. Of those that a mesh axis runs over, the one named last changes fastest.
Arguments:
- tokens: bfloat16 [16384, 3584], P('expert'), may hold values from -6 to 6
- out_grad: bfloat16 [16384, 3584], P('expert'), may hold values from -4 to 4
- route_ids: int32 [16384, 4], P('expert'), may hold values from 0 to 127, all different within a row; in each aligned block of 128 rows (0 to 127, 128 to 255, ...) at most 6 rows name the same one
- route_gates: float32 [16384, 4], P('expert'), may hold values from 0.1 to 1
- w_gate: bfloat16 [128, 3584, 1024], P('expert', None, 'hid'), may hold values from -0.09375 to 0.09375
- w_up: bfloat16 [128, 3584, 1024], P('expert', None, 'hid'), may hold values from -0.09375 to 0.09375
- w_down: bfloat16 [128, 1024, 3584], P('expert', 'hid'), may hold values from -0.1875 to 0.1875
Outputs:
- token_grad: bfloat16 [16384, 3584], P('expert', 'hid')
- gate_grad: bfloat16 [16384, 4], P('expert')
Inputs may be any that keep to these rules, and one draw needn't show every extreme that they name: `route_ids`: each token names 4 different experts. Among the 128 tokens of one index of expert (aligned blocks of rows), no expert is named more than 6 times, a bound that some block reaches.
All inputs are finite; a program needn't handle non-finite values.
Results may differ from a plain program's by a relative error of at most 0.008.
Values may be sent and summed in bfloat16 or wider, within the bound.
No kernel may reach another device: no remote copies, remote signals or barrier semaphores. Data moves between devices by JAX's collectives and lax.ppermute only.
A program may use at most 128 MiB of HBM per device.

v0:
```python
import jax
import jax.numpy as jnp
from jax import lax
from jax.sharding import PartitionSpec as P


def body(tokens, out_grad, route_ids, route_gates, w_gate, w_up, w_down):
    expert_count = lax.axis_size("expert")
    pair_count = lax.axis_size("hid")
    hid_idx = lax.axis_index("hid")
    tok_rows, model_width = tokens.shape
    top_count = route_ids.shape[1]
    capacity = 3 * tok_rows * top_count // (2 * expert_count)
    slot_count = expert_count * capacity
    half_width = model_width // pair_count
    pair_total = tok_rows * top_count
    flat_ids = route_ids.reshape(-1)
    one_hot = (flat_ids[:, None] == jnp.arange(expert_count, dtype=jnp.int32)[None, :]).astype(
        jnp.int32
    )
    earlier = jnp.cumsum(one_hot, axis=0) - one_hot
    slot_index = jnp.sum(earlier * one_hot, axis=1)
    dest_slot = flat_ids * capacity + slot_index
    slot_pair = (
        jnp.zeros((slot_count,), jnp.int32)
        .at[dest_slot]
        .set(jnp.arange(pair_total, dtype=jnp.int32))
    )
    slot_token = slot_pair // top_count
    x_half = lax.dynamic_slice_in_dim(tokens, hid_idx * half_width, half_width, axis=1)
    d_half = lax.dynamic_slice_in_dim(out_grad, hid_idx * half_width, half_width, axis=1)
    send = jnp.stack([x_half[slot_token], d_half[slot_token]], axis=1).reshape(
        expert_count, capacity, 2, half_width
    )
    recv = lax.all_to_all(send, "expert", split_axis=0, concat_axis=0, tiled=True)
    full = lax.all_gather(recv, "hid", axis=3, tiled=True)
    rows_x = full[:, :, 0, :].reshape(slot_count, model_width)
    rows_d = full[:, :, 1, :].reshape(slot_count, model_width)
    gate_mat = w_gate[0]
    up_mat = w_up[0]
    down_mat = w_down[0]
    contract_last = (((1,), (1,)), ((), ()))
    gate_pre = jnp.dot(rows_x, gate_mat, preferred_element_type=jnp.float32)
    up_pre = jnp.dot(rows_x, up_mat, preferred_element_type=jnp.float32)
    grad_hidden = lax.dot_general(
        rows_d, down_mat, contract_last, preferred_element_type=jnp.float32
    )
    sigma_gate = jax.nn.sigmoid(gate_pre)
    act_gate = gate_pre * sigma_gate
    score_part = jnp.sum(act_gate * up_pre * grad_hidden, axis=1)
    grad_gate_pre = (
        grad_hidden * up_pre * sigma_gate * (1.0 + gate_pre * (1.0 - sigma_gate))
    ).astype(jnp.bfloat16)
    grad_up_pre = (grad_hidden * act_gate).astype(jnp.bfloat16)
    grad_part = lax.dot_general(
        grad_gate_pre, gate_mat, contract_last, preferred_element_type=jnp.float32
    ) + lax.dot_general(grad_up_pre, up_mat, contract_last, preferred_element_type=jnp.float32)
    grad_share = lax.psum_scatter(grad_part, "hid", scatter_dimension=1, tiled=True).astype(
        jnp.bfloat16
    )
    score_full = lax.psum(score_part, "hid").astype(jnp.bfloat16)
    back_grad, back_score = (
        lax.all_to_all(
            grad_share.reshape(expert_count, capacity, half_width),
            "expert",
            split_axis=0,
            concat_axis=0,
            tiled=True,
        ),
        lax.all_to_all(
            score_full.reshape(expert_count, capacity),
            "expert",
            split_axis=0,
            concat_axis=0,
            tiled=True,
        ),
    )
    picked = back_grad.reshape(slot_count, half_width)[dest_slot]
    picked = picked.reshape(tok_rows, top_count, half_width).astype(jnp.float32)
    token_grad = jnp.einsum("tkd,tk->td", picked, route_gates).astype(jnp.bfloat16)
    gate_grad = back_score.reshape(slot_count)[dest_slot].reshape(tok_rows, top_count)
    return (token_grad, gate_grad)


def solution(mesh):
    return jax.shard_map(
        body,
        mesh=mesh,
        in_specs=(
            P("expert", None),
            P("expert", None),
            P("expert", None),
            P("expert", None),
            P("expert", None, "hid"),
            P("expert", None, "hid"),
            P("expert", "hid", None),
        ),
        out_specs=(P("expert", "hid"), P("expert", None)),
        check_vma=False,
    )
```

profile of v0, /device:TPU:32, one launch (start us, length us, event | category | flops | bytes accessed | tf_op | source)
XLA Modules:
  0.0 480.9 jit_solution(7994707063346658145)
XLA Ops:
  13.5 4.1 gather_fusion
  17.6 5.4 %stack.9 = bf16[128,6,1,1792]{3,1,0,2:T(8,128)(2,1)} reshape(bf16[768,1792]{1,0:T(8,128)(2,1)} %gather_fusion) | data formatting | bytes 5505024 | tf_op jit(solution)/shard_map/stack | solution.py:32
  23.0 3.2 gather_fusion.1
  28.9 5.1 %pad_maximum_fusion = bf16[128,6,2,1792]{3,1,0,2:T(8,128)(2,1)S(1)} fusion(bf16[128,6,1,1792]{3,1,0,2:T(8,128)(2,1)} %stack.10, bf16[128,6,1,1792]{3,1,0,2:T(8,128)(2,1)} %stack.9), kind=kLoop, calls=%fused_computation.7 | loop fusion | flops 2752512 | bytes 11010048 | tf_op jit(solution)/shard_map/stack | solution.py:32
  34.0 25.1 %copy.20 = bf16[128,6,2,1792]{3,2,1,0:T(2,128)(2,1)S(1)} copy(bf16[128,6,2,1792]{3,1,0,2:T(8,128)(2,1)S(1)} %pad_maximum_fusion) | data formatting | bytes 11010048 | tf_op jit(solution)/shard_map/stack | solution.py:32
  59.2 140.6 %all_to_all.20 = bf16[128,6,2,1792]{3,2,1,0:T(2,128)(2,1)} all-to-all(bf16[128,6,2,1792]{3,2,1,0:T(2,128)(2,1)S(1)} %copy.20), channel_id=1, replica_groups=mesh['expert'=128,'hid'=2] {'expert'}, dimensions={0} | all-to-all | bytes 11010048 | tf_op jit(solution)/shard_map/all_to_all | solution.py:35
  199.9 23.1 %all-gather.2.cloned.1.call-done = bf16[128,6,2,3584]{3,2,1,0:T(2,128)(2,1)} async-done(((bf16[128,6,2,1792]{3,2,1,0:T(2,128)(2,1)}), bf16[128,6,2,3584]{3,2,1,0:T(2,128)(2,1)}) %all-gather.2.cloned.1.call-update) | async-done | bytes 11010064 | tf_op jit(solution)/shard_map/all_gather | solution.py:36
  223.0 59.4 %slice_reduce_fusion.1 = (bf16[128,6,3584]{2,1,0:T(8,128)(2,1)}, bf16[128,6,3584]{2,1,0:T(8,128)(2,1)}) fusion(bf16[128,6,2,3584]{3,2,1,0:T(2,128)(2,1)} %all-gather.2.cloned.1.call-done), kind=kLoop, calls=%fused_computation.6 | loop fusion | bytes 22020096 | tf_op jit(solution)/shard_map/slice | solution.py:38
  282.4 9.7 %reshape_squeeze.7 = bf16[768,3584]{1,0:T(8,128)(2,1)} reshape(bf16[128,6,3584]{2,1,0:T(8,128)(2,1)} %get-tuple-element.7) | data formatting | bytes 11010048 | tf_op jit(solution)/shard_map/reshape;squeeze | solution.py:37
  292.1 6.9 %fusion.2 = f32[768,512]{0,1:T(8,128)S(1)} fusion(bf16[768,3584]{1,0:T(8,128)(2,1)} %reshape_squeeze.7, bf16[1,3584,512]{2,1,0:T(8,128)(2,1)} %param.11), kind=kOutput, calls=%fused_computation.11 | convolution fusion | flops 2818572288 | bytes 10747904 | tf_op jit(solution)/shard_map/dot_general | solution.py:43
  299.0 3.1 fusion.5
  302.0 9.8 %reshape_squeeze.6 = bf16[768,3584]{1,0:T(8,128)(2,1)} reshape(bf16[128,6,3584]{2,1,0:T(8,128)(2,1)} %get-tuple-element.6) | data formatting | bytes 11010048 | tf_op jit(solution)/shard_map/reshape;squeeze | solution.py:38
  311.9 7.0 %multiply_reduce_fusion = (f32[768]{0:T(1024)S(1)}, f32[768,512]{0,1:T(8,128)S(1)}) fusion(f32[768,512]{0,1:T(8,128)S(1)} %fusion.5, f32[768,512]{0,1:T(8,128)S(1)} %fusion.2, bf16[768,3584]{1,0:T(8,128)(2,1)} %reshape_squeeze.6, bf16[1,512,3584]{2,1,0:T(8,128)(2,1)} %param.13), kind=kOutput, calls=%fused_computation.18 | convolution fusion | flops 2821324032 | bytes 13896704 | tf_op jit(solution)/shard_map/dot_general | solution.py:45
  318.9 3.6 fusion
  322.5 7.9 %convolution_add_fusion = f32[768,3584]{1,0:T(8,128)} fusion(f32[768,3584]{1,0:T(8,128)S(1)} %fusion, bf16[1,3584,512]{2,1,0:T(8,128)(2,1)} %param.12, f32[768,512]{0,1:T(8,128)S(1)} %get-tuple-element.9, f32[768,512]{0,1:T(8,128)S(1)} %fusion.2), kind=kOutput, calls=%fused_computation.8 | convolution fusion | flops 2823684096 | bytes 28835840 | tf_op jit(solution)/shard_map/dot_general | solution.py:57
  333.7 13.7 %all-to-all-start.2 = ((bf16[128,1,6]{2,1,0:T(2,128)(2,1)}), bf16[128,1,6]{2,1,0:T(2,128)(2,1)S(1)}, u32[]{:S(2)}, u32[]{:S(2)}) async-start(bf16[128,1,6]{2,1,0:T(2,128)(2,1)} %all_to_all.16), calls=%async_computation.3 | async-start | bytes 131072 | tf_op jit(solution)/shard_map/all_to_all | solution.py:70
  347.4 8.2 %reduce-scatter.2.cloned.1.call-done = f32[768,1792]{1,0:T(8,128)} async-done(((f32[768,3584]{1,0:T(8,128)}), f32[768,1792]{1,0:T(8,128)}) %reduce-scatter.2.cloned.1.call-update) | async-done | bytes 5505040 | tf_op jit(solution)/shard_map/reduce_scatter | solution.py:58
  355.6 2.8 convert_element_type.27
  361.1 14.6 %all-to-all-start.1 = ((bf16[128,6,1792]{2,1,0:T(8,128)(2,1)}), bf16[128,6,1792]{2,1,0:T(8,128)(2,1)}, u32[]{:S(2)}, u32[]{:S(2)}) async-start(bf16[128,6,1792]{2,1,0:T(8,128)(2,1)} %reshape.76), calls=%async_computation.2 | async-start | bytes 7340032 | tf_op jit(solution)/shard_map/all_to_all | solution.py:63
  376.3 3.5 gather_fusion.3
  380.6 81.1 %all-to-all-done.1 = bf16[128,6,1792]{2,1,0:T(8,128)(2,1)} async-done(((bf16[128,6,1792]{2,1,0:T(8,128)(2,1)}), bf16[128,6,1792]{2,1,0:T(8,128)(2,1)}, u32[]{:S(2)}, u32[]{:S(2)}) %all-to-all-start.1) | async-done | bytes 2752544 | tf_op jit(solution)/shard_map/all_to_all | solution.py:63
  461.7 4.0 reshape.77
  465.6 3.2 gather_fusion.2
  468.8 3.1 reshape.78
  (46 shorter events, 18.2 us)
Async XLA Ops:
  7.2 215.9 %all-gather.2.cloned.1.call-start = ((), (), s32[]{:S(2)}) async-start(), calls=%async_computation.4 | async-start | bytes 16515072 | tf_op jit(solution)/shard_map/all_gather | solution.py:36
  199.8 155.8 %reduce-scatter.2.cloned.1.call-start = ((), (), s32[]{:S(2)}) async-start(), calls=%async_computation.5 | async-start | bytes 16515072 | tf_op jit(solution)/shard_map/reduce_scatter | solution.py:58
  292.1 6.9 %copy-start = (bf16[768,3584]{1,0:T(8,128)(2,1)S(1)}, bf16[768,3584]{1,0:T(8,128)(2,1)}, u32[]{:S(2)}) copy-start(bf16[768,3584]{1,0:T(8,128)(2,1)} %reshape_squeeze.7) | copy-start | bytes 16515076
  292.1 6.9 %copy-start.2 = (bf16[1,3584,512]{2,1,0:T(8,128)(2,1)S(1)}, bf16[1,3584,512]{2,1,0:T(8,128)(2,1)}, u32[]{:S(2)}) copy-start(bf16[1,3584,512]{2,1,0:T(8,128)(2,1)} %param.12) | copy-start | bytes 11010052
  311.9 7.0 %copy-start.1 = (bf16[1,3584,512]{2,1,0:T(8,128)(2,1)S(1)}, bf16[1,3584,512]{2,1,0:T(8,128)(2,1)}, u32[]{:S(2)}) copy-start(bf16[1,3584,512]{2,1,0:T(8,128)(2,1)} %param.11) | copy-start | bytes 11010052
  333.7 27.4 %all-to-all-start.2 = ((bf16[128,1,6]{2,1,0:T(2,128)(2,1)}), bf16[128,1,6]{2,1,0:T(2,128)(2,1)S(1)}, u32[]{:S(2)}, u32[]{:S(2)}) async-start(bf16[128,1,6]{2,1,0:T(2,128)(2,1)} %all_to_all.16), calls=%async_computation.3 | async-start | bytes 131072 | tf_op jit(solution)/shard_map/all_to_all | solution.py:70
  361.1 14.6 %copy-start.3 = (f32[128,4]{0,1:T(4,128)S(1)}, f32[128,4]{0,1:T(4,128)}, u32[]{:S(2)}) copy-start(f32[128,4]{0,1:T(4,128)} %param.10) | copy-start | bytes 6148
  361.1 100.5 %all-to-all-start.1 = ((bf16[128,6,1792]{2,1,0:T(8,128)(2,1)}), bf16[128,6,1792]{2,1,0:T(8,128)(2,1)}, u32[]{:S(2)}, u32[]{:S(2)}) async-start(bf16[128,6,1792]{2,1,0:T(8,128)(2,1)} %reshape.76), calls=%async_computation.2 | async-start | bytes 7340032 | tf_op jit(solution)/shard_map/all_to_all | solution.py:63
Sparse Core Ops, SparseCore 0:
  200.0 23.0 all-gather.1
  330.6 24.9 reduce-scatter.1
where the time goes:
time: 490 us; the launch traced here: 481 us
  local copies, waits for them, and re-layouts  144 us (29%)
  blocking collectives  143 us (29%)
  waiting for transfers between devices  112 us (23%)
  matrix products  29.5 us (6%)
  starting transfers between devices  28.4 us (6%)
  between operations  14.5 us (3%)
  other arithmetic  9.33 us (2%)
    all_to_all x1, blocking collectives, body(): lax.all_to_all(send, 'expert', split_axis=0, concat_axis=0, tiled=True)  141 us
    all_to_all x1, waiting for transfers between devices, body(): lax.all_to_all(grad_share.reshape(expert_count, capacity, half_width), 'e...  81.1 us
    slice x1, local copies, waits for them, and re-layouts, body(): rows_d = full[:, :, 1, :].reshape(slot_count, model_width)  59.4 us
    another operation x3, local copies, waits for them, and re-layouts, body(): jnp.stack([x_half[slot_token], d_half[slot_token]], axis=1)  33.3 us
    all_gather x1, waiting for transfers between devices, body(): full = lax.all_gather(recv, 'hid', axis=3, tiled=True)  23.1 us
    all_to_all x1, starting transfers between devices, body(): lax.all_to_all(grad_share.reshape(expert_count, capacity, half_width), 'e...  14.6 us
    all_to_all x1, starting transfers between devices, body(): lax.all_to_all(score_full.reshape(expert_count, capacity), 'expert', spli...  13.7 us
    another operation x1, local copies, waits for them, and re-layouts, body(): rows_d = full[:, :, 1, :].reshape(slot_count, model_width)  9.82 us
  transfers between devices with their start and end apart: 4, of which 3 were waited for; matrix products, arithmetic and copies ran while one was open for 2% of the time, Pallas kernels for 0%

commit v1 on v0

--- a/solution.py
+++ b/solution.py
@@ -33,7 +33,9 @@
         expert_count, capacity, 2, half_width
     )
     recv = lax.all_to_all(send, "expert", split_axis=0, concat_axis=0, tiled=True)
-    full = lax.all_gather(recv, "hid", axis=3, tiled=True)
+    full = jnp.concatenate(
+        lax.all_to_all(jnp.stack([recv] * lax.axis_size("hid")), "hid", 0, 0), axis=3
+    )
     rows_x = full[:, :, 0, :].reshape(slot_count, model_width)
     rows_d = full[:, :, 1, :].reshape(slot_count, model_width)
     gate_mat = w_gate[0]

time: 490 us -> 464 us (0.947); the launches traced: 481 us -> 462 us
  waiting for transfers between devices: 112 us -> 89.5 us
  blocking collectives: 143 us -> 157 us
  local copies, waits for them, and re-layouts: 144 us -> 131 us
  other arithmetic: 9.33 us -> 19.8 us
  starting transfers between devices: 28.4 us -> 21.2 us
    slice x1 -> x2, local copies, waits for them, and re-layouts: 59.4 us -> 19.1 us  [body(): rows_d = full[:, :, 1, :].reshape(slot_count, model_width)]
    all_gather x1 -> x0, waiting for transfers between devices: 23.1 us -> none  [body(): full = lax.all_gather(recv, 'hid', axis=3, tiled=True)]
    all_to_all x0 -> x1, local copies, waits for them, and re-layouts: none -> 14.9 us  [body(): lax.all_to_all(jnp.stack([recv] * lax.axis_size('hid')), 'hid', 0, 0)]
    all_to_all x0 -> x1, blocking collectives: none -> 14.1 us  [body(): lax.all_to_all(jnp.stack([recv] * lax.axis_size('hid')), 'hid', 0, 0)]
    another operation x3 -> x4, other arithmetic: 0.26 us -> 10.7 us  [the longest x1 10.5 us: body(): jnp.stack([recv] * lax.axis_size('hid'))]
    slice x0 -> x1, local copies, waits for them, and re-layouts: none -> 10.1 us  [body(): rows_x = full[:, :, 0, :].reshape(slot_count, model_width)]
    all_to_all x1, starting transfers between devices: 13.7 us -> 6.94 us  [body(): lax.all_to_all(score_full.reshape(expert_count, capacity), 'expert', spli...]
  transfers between devices with their start and end apart: 4 -> 3, of which waited for: 3 -> 2; matrix products, arithmetic and copies ran while one was open for 2% -> 2% of each run, Pallas kernels for 0% -> 0%
where the time goes in v1:
time: 464 us; the launch traced here: 462 us
  blocking collectives  157 us (34%)
  local copies, waits for them, and re-layouts  131 us (28%)
  waiting for transfers between devices  89.5 us (19%)
  matrix products  29.5 us (6%)
  starting transfers between devices  21.2 us (5%)
  other arithmetic  19.8 us (4%)
  between operations  14.3 us (3%)
    all_to_all x1, blocking collectives, body(): lax.all_to_all(send, 'expert', split_axis=0, concat_axis=0, tiled=True)  141 us
    all_to_all x1, waiting for transfers between devices, body(): lax.all_to_all(grad_share.reshape(expert_count, capacity, half_width), 'e...  81.2 us
    another operation x3, local copies, waits for them, and re-layouts, body(): jnp.stack([x_half[slot_token], d_half[slot_token]], axis=1)  33.3 us
    slice x2, local copies, waits for them, and re-layouts, body(): rows_d = full[:, :, 1, :].reshape(slot_count, model_width)  19.1 us
    all_to_all x1, local copies, waits for them, and re-layouts, body(): lax.all_to_all(jnp.stack([recv] * lax.axis_size('hid')), 'hid', 0, 0)  14.9 us
    all_to_all x1, starting transfers between devices, body(): lax.all_to_all(grad_share.reshape(expert_count, capacity, half_width), 'e...  14.2 us
    all_to_all x1, blocking collectives, body(): lax.all_to_all(jnp.stack([recv] * lax.axis_size('hid')), 'hid', 0, 0)  14.1 us
    another operation x1, other arithmetic, body(): jnp.stack([recv] * lax.axis_size('hid'))  10.5 us
  transfers between devices with their start and end apart: 3, of which 2 were waited for; matrix products, arithmetic and copies ran while one was open for 2% of the time, Pallas kernels for 0%

profile of v1, /device:TPU:32, one launch (start us, length us, event | category | flops | bytes accessed | tf_op | source)
XLA Modules:
  0.0 462.1 jit_solution(13122906355646345245)
XLA Ops:
  13.5 4.1 gather_fusion
  17.6 5.4 %stack.16 = bf16[128,6,1,1792]{3,1,0,2:T(8,128)(2,1)} reshape(bf16[768,1792]{1,0:T(8,128)(2,1)} %gather_fusion) | data formatting | bytes 5505024 | tf_op jit(solution)/shard_map/stack | solution.py:32
  23.0 3.2 gather_fusion.1
  28.9 5.1 %pad_maximum_fusion.1 = bf16[128,6,2,1792]{3,1,0,2:T(8,128)(2,1)S(1)} fusion(bf16[128,6,1,1792]{3,1,0,2:T(8,128)(2,1)} %stack.17, bf16[128,6,1,1792]{3,1,0,2:T(8,128)(2,1)} %stack.16), kind=kLoop, calls=%fused_computation.6 | loop fusion | flops 2752512 | bytes 11010048 | tf_op jit(solution)/shard_map/stack | solution.py:32
  34.0 25.1 %copy.23 = bf16[128,6,2,1792]{3,2,1,0:T(2,128)(2,1)S(1)} copy(bf16[128,6,2,1792]{3,1,0,2:T(8,128)(2,1)S(1)} %pad_maximum_fusion.1) | data formatting | bytes 11010048 | tf_op jit(solution)/shard_map/stack | solution.py:32
  59.2 140.5 %all_to_all.25 = bf16[128,6,2,1792]{3,2,1,0:T(2,128)(2,1)S(1)} all-to-all(bf16[128,6,2,1792]{3,2,1,0:T(2,128)(2,1)S(1)} %copy.23), channel_id=1, replica_groups=mesh['expert'=128,'hid'=2] {'expert'}, dimensions={0} | all-to-all | bytes 11010048 | tf_op jit(solution)/shard_map/all_to_all | solution.py:35
  199.7 10.5 %pad_maximum_fusion = bf16[2,128,6,2,1792]{4,3,2,1,0:T(2,128)(2,1)S(1)} fusion(bf16[1,128,6,2,1792]{4,3,2,1,0:T(2,128)(2,1)S(1)} %bitcast.48), kind=kLoop, calls=%fused_computation.5 | loop fusion | flops 5505024 | bytes 16515072 | tf_op jit(solution)/shard_map/stack | solution.py:37
  212.8 14.1 %all_to_all.26 = bf16[2,128,6,2,1792]{4,1,3,2,0:T(8,128)(2,1)} all-to-all(bf16[2,128,6,2,1792]{4,1,3,2,0:T(8,128)(2,1)S(1)} %copy.24), channel_id=1, replica_groups=mesh['expert'=128,'hid'=2] {'hid'}, dimensions={0} | all-to-all | bytes 22020096 | tf_op jit(solution)/shard_map/all_to_all | solution.py:37
  226.8 14.9 %copy.25 = bf16[2,128,6,2,1792]{1,4,0,3,2:T(8,128)(2,1)} copy(bf16[2,128,6,2,1792]{4,1,3,2,0:T(8,128)(2,1)} %all_to_all.26) | data formatting | bytes 22020096 | tf_op jit(solution)/shard_map/all_to_all | solution.py:37
  241.7 8.9 %fusion.23 = (bf16[128,6,1,3584]{0,3,2,1:T(8,128)(2,1)}, bf16[128,6,1,3584]{0,3,2,1:T(8,128)(2,1)}) fusion(bf16[128,6,2,3584]{0,3,2,1:T(8,128)(2,1)} %bitcast.47), kind=kLoop, calls=%fused_computation.52 | loop fusion | bytes 22020096 | tf_op jit(solution)/shard_map/slice | solution.py:40
  250.6 10.1 %copy.27 = bf16[128,6,1,3584]{3,1,0,2:T(8,128)(2,1)} copy(bf16[128,6,1,3584]{0,3,2,1:T(8,128)(2,1)} %get-tuple-element.7) | data formatting | bytes 11010048 | tf_op jit(solution)/shard_map/slice | solution.py:39
  260.8 9.7 %reshape_squeeze.7 = bf16[768,3584]{1,0:T(8,128)(2,1)} reshape(bf16[128,6,1,3584]{3,1,0,2:T(8,128)(2,1)} %copy.27) | data formatting | bytes 11010048 | tf_op jit(solution)/shard_map/reshape;squeeze | solution.py:39
  270.4 6.9 %fusion.2 = f32[768,512]{0,1:T(8,128)S(1)} fusion(bf16[768,3584]{1,0:T(8,128)(2,1)} %reshape_squeeze.7, bf16[1,3584,512]{2,1,0:T(8,128)(2,1)} %param.11), kind=kOutput, calls=%fused_computation.10 | convolution fusion | flops 2818572288 | bytes 10747904 | tf_op jit(solution)/shard_map/dot_general | solution.py:45
  280.4 10.1 %copy.26 = bf16[128,6,1,3584]{3,1,0,2:T(8,128)(2,1)} copy(bf16[128,6,1,3584]{0,3,2,1:T(8,128)(2,1)} %get-tuple-element.6) | data formatting | bytes 11010048 | tf_op jit(solution)/shard_map/slice | solution.py:40
  290.5 9.7 %reshape_squeeze.6 = bf16[768,3584]{1,0:T(8,128)(2,1)} reshape(bf16[128,6,1,3584]{3,1,0,2:T(8,128)(2,1)} %copy.26) | data formatting | bytes 11010048 | tf_op jit(solution)/shard_map/reshape;squeeze | solution.py:40
  300.2 7.0 %multiply_reduce_fusion = (f32[768]{0:T(1024)S(1)}, f32[768,512]{0,1:T(8,128)S(1)}) fusion(f32[768,512]{0,1:T(8,128)S(1)} %fusion.5, f32[768,512]{0,1:T(8,128)S(1)} %fusion.2, bf16[768,3584]{1,0:T(8,128)(2,1)} %reshape_squeeze.6, bf16[1,512,3584]{2,1,0:T(8,128)(2,1)} %param.13), kind=kOutput, calls=%fused_computation.17 | convolution fusion | flops 2821324032 | bytes 13896704 | tf_op jit(solution)/shard_map/dot_general | solution.py:47
  307.2 3.6 fusion
  310.8 7.9 %convolution_add_fusion = f32[768,3584]{1,0:T(8,128)} fusion(f32[768,3584]{1,0:T(8,128)S(1)} %fusion, bf16[1,3584,512]{2,1,0:T(8,128)(2,1)} %param.12, f32[768,512]{0,1:T(8,128)S(1)} %get-tuple-element.9, f32[768,512]{0,1:T(8,128)S(1)} %fusion.2), kind=kOutput, calls=%fused_computation.7 | convolution fusion | flops 2823684096 | bytes 28835840 | tf_op jit(solution)/shard_map/dot_general | solution.py:59
  322.1 6.9 %all-to-all-start.3 = ((bf16[128,1,6]{2,1,0:T(2,128)(2,1)}), bf16[128,1,6]{2,1,0:T(2,128)(2,1)S(1)}, u32[]{:S(2)}, u32[]{:S(2)}) async-start(bf16[128,1,6]{2,1,0:T(2,128)(2,1)} %all_to_all.20), calls=%async_computation.4 | async-start | bytes 131072 | tf_op jit(solution)/shard_map/all_to_all | solution.py:72
  329.0 8.2 %reduce-scatter.2.cloned.1.call-done = f32[768,1792]{1,0:T(8,128)} async-done(((f32[768,3584]{1,0:T(8,128)}), f32[768,1792]{1,0:T(8,128)}) %reduce-scatter.2.cloned.1.call-update) | async-done | bytes 5505040 | tf_op jit(solution)/shard_map/reduce_scatter | solution.py:60
  342.7 14.2 %all-to-all-start.2 = ((bf16[128,6,1792]{2,1,0:T(8,128)(2,1)}), bf16[128,6,1792]{2,1,0:T(8,128)(2,1)}, u32[]{:S(2)}, u32[]{:S(2)}) async-start(bf16[128,6,1792]{2,1,0:T(8,128)(2,1)} %reshape.84), calls=%async_computation.3 | async-start | bytes 7340032 | tf_op jit(solution)/shard_map/all_to_all | solution.py:65
  357.5 3.5 gather_fusion.3
  361.8 81.2 %all-to-all-done.2 = bf16[128,6,1792]{2,1,0:T(8,128)(2,1)} async-done(((bf16[128,6,1792]{2,1,0:T(8,128)(2,1)}), bf16[128,6,1792]{2,1,0:T(8,128)(2,1)}, u32[]{:S(2)}, u32[]{:S(2)}) %all-to-all-start.2) | async-done | bytes 2752544 | tf_op jit(solution)/shard_map/all_to_all | solution.py:65
  443.0 4.0 reshape.85
  (49 shorter events, 32.9 us)
Async XLA Ops:
  7.2 330.0 %reduce-scatter.2.cloned.1.call-start = ((), (), s32[]{:S(2)}) async-start(), calls=%async_computation.5 | async-start | bytes 16515072 | tf_op jit(solution)/shard_map/reduce_scatter | solution.py:60
  270.4 6.9 %copy-start = (bf16[768,3584]{1,0:T(8,128)(2,1)S(1)}, bf16[768,3584]{1,0:T(8,128)(2,1)}, u32[]{:S(2)}) copy-start(bf16[768,3584]{1,0:T(8,128)(2,1)} %reshape_squeeze.7) | copy-start | bytes 16515076
  270.4 6.9 %copy-start.2 = (bf16[1,3584,512]{2,1,0:T(8,128)(2,1)S(1)}, bf16[1,3584,512]{2,1,0:T(8,128)(2,1)}, u32[]{:S(2)}) copy-start(bf16[1,3584,512]{2,1,0:T(8,128)(2,1)} %param.12) | copy-start | bytes 11010052
  300.2 7.0 %copy-start.1 = (bf16[1,3584,512]{2,1,0:T(8,128)(2,1)S(1)}, bf16[1,3584,512]{2,1,0:T(8,128)(2,1)}, u32[]{:S(2)}) copy-start(bf16[1,3584,512]{2,1,0:T(8,128)(2,1)} %param.11) | copy-start | bytes 11010052
  322.1 20.7 %all-to-all-start.3 = ((bf16[128,1,6]{2,1,0:T(2,128)(2,1)}), bf16[128,1,6]{2,1,0:T(2,128)(2,1)S(1)}, u32[]{:S(2)}, u32[]{:S(2)}) async-start(bf16[128,1,6]{2,1,0:T(2,128)(2,1)} %all_to_all.20), calls=%async_computation.4 | async-start | bytes 131072 | tf_op jit(solution)/shard_map/all_to_all | solution.py:72
  342.7 14.3 %copy-start.3 = (f32[128,4]{0,1:T(4,128)S(1)}, f32[128,4]{0,1:T(4,128)}, u32[]{:S(2)}) copy-start(f32[128,4]{0,1:T(4,128)} %param.10) | copy-start | bytes 6148
  342.7 100.3 %all-to-all-start.2 = ((bf16[128,6,1792]{2,1,0:T(8,128)(2,1)}), bf16[128,6,1792]{2,1,0:T(8,128)(2,1)}, u32[]{:S(2)}, u32[]{:S(2)}) async-start(bf16[128,6,1792]{2,1,0:T(8,128)(2,1)} %reshape.84), calls=%async_computation.3 | async-start | bytes 7340032 | tf_op jit(solution)/shard_map/all_to_all | solution.py:65
Sparse Core Ops, SparseCore 0:
  318.9 18.2 reduce-scatter.1
